TPU v7x, 512 devices: a whole 4x8x8 slice. The times are simulated.
512 devices in a mesh: dp: 64 (over z, y_hi, core), mp: 8 (over x, y_lo).
Axes of the slice: x: 4, y: 8 (y_hi: 4, y_lo: 2; y = y_hi * 2 + y_lo), z: 8, core: 2. Of those that a mesh axis runs over, the one named last changes fastest.
Arguments:
- queries: bfloat16 [32768, 8192], P('dp', 'mp'), may hold values from -45 to 45
- key_rows: bfloat16 [32768, 1024], P('dp', 'mp'), may hold values from -4 to 4
- value_rows: bfloat16 [32768, 1024], P('dp', 'mp'), may hold values from -6 to 6
- landmark_index: int32 [512], P('dp'), may hold values from 0 to 32767, as said below
- radius_in: float32 [512], replicated, may hold values from 0.5 to 4
- radius_out: float32 [512], replicated, may hold values from 0.02 to 0.5
Outputs:
- cross_covariance: float32 [512, 512], P('mp', 'dp')
Inputs may be any that keep to these rules, and one draw needn't show every extreme that they name: `landmark_index`: the 8 landmarks held by index d of dp name distinct tokens of sequence d, that is, positions d * 512 to (d + 1) * 512 - 1.
All inputs are finite; a program needn't handle non-finite values.
Results may differ from a plain program's by a relative error of at most 0.003.
Values may be sent and summed in bfloat16 or wider, within the bound.
No kernel may reach another device: no remote copies, remote signals or barrier semaphores. Data moves between devices by JAX's collectives and lax.ppermute only.
A program may use at most 64 MiB of HBM per device.

v0:
```python
import functools
import math
import jax
import jax.numpy as jnp
from jax import lax
from jax.sharding import PartitionSpec as P

D = 8192
HEAD_DIM = 128
EPSILON = 1e-06


def attend_head(queries, key_rows, value_rows, group_size, head_index):
    query_head = lax.dynamic_slice_in_dim(queries, head_index * HEAD_DIM, HEAD_DIM, 1)
    scores = lax.dot_general(
        query_head, key_rows, (((1,), (1,)), ((), ())), preferred_element_type=jnp.float32
    ) / math.sqrt(HEAD_DIM)
    length = queries.shape[0]
    row_position = lax.broadcasted_iota(jnp.int32, (length, length), 0)
    column_position = lax.broadcasted_iota(jnp.int32, (length, length), 1)
    scores = jnp.where(column_position <= row_position, scores, -jnp.inf)
    weights = jax.nn.softmax(scores, axis=-1).astype(jnp.bfloat16)
    return jnp.dot(weights, value_rows, preferred_element_type=jnp.float32).astype(jnp.bfloat16)


def squares_by_row(matrix):
    return jnp.sum(jnp.square(matrix.astype(jnp.float32)), axis=-1)


def inner_rows(left, right):
    return lax.dot_general(
        left, right, (((1,), (1,)), ((), ())), preferred_element_type=jnp.float32
    )


def inner_columns(left, right):
    return lax.dot_general(
        left, right, (((0,), (0,)), ((), ())), preferred_element_type=jnp.float32
    )


def center(features, totals, token_count):
    return (features.astype(jnp.float32) - totals / token_count).astype(jnp.bfloat16)


def shards(queries, key_rows, value_rows, landmark_index, radius_in, radius_out):
    length = queries.shape[0]
    heads_local = queries.shape[1] // HEAD_DIM
    group_size = heads_local // (key_rows.shape[1] // HEAD_DIM)
    per_head = lax.map(
        functools.partial(attend_head, queries, key_rows, value_rows, group_size),
        jnp.arange(heads_local, dtype=jnp.int32),
    )
    attended = jnp.transpose(per_head, (1, 0, 2)).reshape(length, heads_local * HEAD_DIM)
    landmarks = radius_in.shape[0]
    model_index = lax.axis_index("mp")
    data_index = lax.axis_index("dp")
    row_share = landmarks // lax.axis_size("mp")
    column_share = landmarks // lax.axis_size("dp")
    token_count = length * lax.axis_size("dp")
    widths = jnp.stack([radius_in, radius_out])
    own_rows = landmark_index % length
    landmark_rows = jnp.stack(
        [jnp.take(queries, own_rows, axis=0), jnp.take(attended, own_rows, axis=0)]
    )
    row_norms = jnp.stack([squares_by_row(queries), squares_by_row(attended)])
    landmark_piece = lax.all_gather(landmark_rows, "dp", axis=1, tiled=True)
    mark_norms = squares_by_row(landmark_piece)
    cross = jnp.stack(
        [inner_rows(queries, landmark_piece[0]), inner_rows(attended, landmark_piece[1])]
    )
    distance_part = row_norms[:, :, None] + mark_norms[:, None, :] - 2.0 * cross
    distance = lax.psum(distance_part, "mp")
    features = jnp.exp(-distance / (D * widths[:, None, :])).astype(jnp.bfloat16)
    row_features = lax.dynamic_slice_in_dim(features[0], model_index * row_share, row_share, 1)
    column_features = features[1]
    row_total, column_total = lax.psum(
        (
            jnp.sum(row_features.astype(jnp.float32), axis=0),
            jnp.sum(column_features.astype(jnp.float32), axis=0),
        ),
        "dp",
    )
    rows_centered = center(row_features, row_total[None, :], token_count)
    columns_centered = center(column_features, column_total[None, :], token_count)
    second = inner_columns(rows_centered, columns_centered)
    row_spread = jnp.sum(jnp.square(rows_centered.astype(jnp.float32)), axis=0)
    column_spread = jnp.sum(jnp.square(columns_centered.astype(jnp.float32)), axis=0)
    second, row_spread, column_spread = lax.psum((second, row_spread, column_spread), "dp")
    own_block = lax.dynamic_slice_in_dim(second, data_index * column_share, column_share, 1)
    column_spread = lax.dynamic_slice_in_dim(
        column_spread, data_index * column_share, column_share, 0
    )
    covariance = own_block / token_count
    spread_rows = row_spread / token_count
    spread_columns = column_spread / token_count
    return covariance / jnp.sqrt(
        (spread_rows + EPSILON)[:, None] * (spread_columns + EPSILON)[None, :]
    )


def solution(mesh):
    return jax.shard_map(
        shards,
        mesh=mesh,
        in_specs=(P("dp", "mp"), P("dp", "mp"), P("dp", "mp"), P("dp"), P(), P()),
        out_specs=P("mp", "dp"),
        check_vma=False,
    )
```

profile of v0, /device:TPU:1, one launch (start us, length us, event | category | flops | bytes accessed | tf_op | source)
XLA Modules:
  0.0 903.9 jit_solution(17541337728010904406)
XLA Ops:
  6.5 0.7 compare_and_fusion
  7.2 1.9 gather_fusion
  9.2 26.6 %while.10 = (s32[]{:T(128)}, bf16[8,512,128]{2,1,0:T(8,128)(2,1)S(1)}, s32[8]{0:T(128)S(1)}, bf16[512,1024]{1,0:T(8,128)(2,1)}, bf16[512,128]{1,0:T(8,128)(2,1)}...) while((s32[]{:T(128)}, bf16[8,512,128]{2,1,0:T(8,128)(2,1)S(1)}, ...), condition=%wide.region_4.5_spmd, body=%wide.region_1.4_spmd.sunk | while | flops 136641536 | bytes 4204747 | solution.py:50
  9.2 0.7 dynamic_slice.34
  10.6 1.3 fusion.39
  12.5 0.7 dynamic_slice.34
  13.9 1.3 fusion.39
  17.2 1.3 fusion.39
  20.5 1.3 fusion.39
  23.9 1.3 fusion.39
  27.2 1.3 fusion.39
  30.5 1.3 fusion.39
  33.9 1.3 fusion.39
  37.9 89.6 %all-gather.2.cloned.1.call-done = bf16[2,512,1024]{2,1,0:T(8,128)(2,1)} async-done(((bf16[2,8,1024]{2,1,0:T(8,128)(2,1)}), bf16[2,512,1024]{2,1,0:T(8,128)(2,1)}) %all-gather.2.cloned.1.call-update) | async-done | bytes 2097168 | tf_op jit(solution)/shard_map/all_gather | solution.py:67
  127.4 2.1 convolution_bitcast_fusion
  130.1 0.8 convolution_bitcast_fusion.1
  130.8 1.6 fusion.8
  133.1 110.2 %all-reduce.5.cloned.1.call-done = f32[2,512,512]{1,2,0:T(8,128)} async-done(((f32[2,512,512]{1,2,0:T(8,128)}), f32[2,512,512]{1,2,0:T(8,128)}) %all-reduce.5.cloned.1.call-update) | async-done | bytes 2097168 | tf_op jit(solution)/shard_map/psum | solution.py:73
  243.3 2.0 exponential_convert_fusion
  245.7 139.0 %all-reduce.1 = (f32[512]{0:T(512)S(1)}, f32[64]{0:T(128)S(1)}) all-reduce(f32[512]{0:T(512)S(1)} %convert_reduce_fusion, f32[64]{0:T(128)S(1)} %convert_reduce_fusion.1), channel_id=1, replica_groups=mesh['dp'=64,'mp'=8] {'dp'}, use_global_device_ids=true, to_apply=%region_11.13 | all-reduce | flops 576 | bytes 4608 | tf_op jit(solution)/shard_map/psum | solution.py:77
  384.9 1.1 fusion.13
  386.3 143.5 %all-reduce = (f32[512]{0:T(512)S(1)}, f32[64]{0:T(128)S(1)}) all-reduce(f32[512]{0:T(512)S(1)} %multiply_reduce_fusion.3, f32[64]{0:T(128)S(1)} %multiply_reduce_fusion.4), channel_id=1, replica_groups=mesh['dp'=64,'mp'=8] {'dp'}, use_global_device_ids=true, to_apply=%region_16.18 | all-reduce | flops 576 | bytes 4608 | tf_op jit(solution)/shard_map/psum | solution.py:89
  529.9 366.1 %all-reduce.7.cloned.1.call-done = f32[64,512]{0,1:T(8,128)} async-done(((f32[64,512]{0,1:T(8,128)}), f32[64,512]{0,1:T(8,128)}) %all-reduce.7.cloned.1.call-update) | async-done | bytes 131088 | tf_op jit(solution)/shard_map/psum | solution.py:89
  896.0 1.3 rsqrt_multiply_fusion
  (73 shorter events, 13.2 us)
Async XLA Ops:
  6.5 120.9 %all-gather.2.cloned.1.call-start = ((), (), s32[]{:S(2)}) async-start(), calls=%async_computation | async-start | bytes 2129920 | tf_op jit(solution)/shard_map/all_gather | solution.py:67
  9.2 2.9 copy-start.4
  12.5 2.9 copy-start.4
  15.8 2.9 copy-start.4
  19.2 2.9 copy-start.4
  22.5 2.9 copy-start.4
  25.8 2.9 copy-start.4
  29.1 2.9 copy-start.4
  32.5 2.9 copy-start.4
  35.8 1.5 copy-start.1
  37.2 206.1 %all-reduce.5.cloned.1.call-start = ((), (), s32[]{:S(2)}) async-start(), calls=%async_computation.1 | async-start | bytes 4194304 | tf_op jit(solution)/shard_map/psum | solution.py:73
  127.4 2.1 copy-start
  132.4 0.7 copy-start.2
  132.4 0.7 copy-start.3
  132.4 763.6 %all-reduce.7.cloned.1.call-start = ((), (), s32[]{:S(2)}) async-start(), calls=%async_computation.2 | async-start | bytes 524288 | tf_op jit(solution)/shard_map/psum | solution.py:89
Sparse Core Ops, SparseCore 0:
  37.4 90.0 all-gather.1
  132.6 110.7 all-reduce.4
  386.4 509.5 all-reduce.6
where the time goes:
time: 904 us
  waiting for transfers between devices  566 us (63%)
  blocking collectives  283 us (31%)
  matrix products  17.8 us (2%)
  between operations  13.2 us (1%)
  other arithmetic  9.8 us (1%)
    psum x1, waiting for transfers between devices, shards(): lax.psum((second, row_spread, column_spread), 'dp')  366 us
    psum x1, blocking collectives, shards(): lax.psum((second, row_spread, column_spread), 'dp')  144 us
    psum x1, blocking collectives, shards(): lax.psum((jnp.sum(row_features.astype(jnp.float32), axis=0), jnp.sum(colu...  139 us
    psum x1, waiting for transfers between devices, shards(): distance = lax.psum(distance_part, 'mp')  110 us
    all_gather x1, waiting for transfers between devices, shards(): landmark_piece = lax.all_gather(landmark_rows, 'dp', axis=1, tiled=True)  89.6 us
  transfers between devices with their start and end apart: 3, of which 3 were waited for; matrix products, arithmetic and copies ran while one was open for 0% of the time, Pallas kernels for 0%

commit v1 on v0

--- a/solution.py
+++ b/solution.py
@@ -70,7 +70,7 @@
         [inner_rows(queries, landmark_piece[0]), inner_rows(attended, landmark_piece[1])]
     )
     distance_part = row_norms[:, :, None] + mark_norms[:, None, :] - 2.0 * cross
-    distance = lax.psum(distance_part, "mp")
+    distance = jnp.sum(lax.all_gather(distance_part, "mp"), axis=0)
     features = jnp.exp(-distance / (D * widths[:, None, :])).astype(jnp.bfloat16)
     row_features = lax.dynamic_slice_in_dim(features[0], model_index * row_share, row_share, 1)
     column_features = features[1]

time: 904 us -> 1130 us (1.25)
  waiting for transfers between devices: 566 us -> 783 us
    all_gather x0 -> x1, waiting for transfers between devices: none -> 326 us  [shards(): distance = jnp.sum(lax.all_gather(distance_part, 'mp'), axis=0)]
    psum x1 -> x0, waiting for transfers between devices: 110 us -> none  [shards(): distance = lax.psum(distance_part, 'mp')]
where the time goes in v1:
time: 1130 us
  waiting for transfers between devices  783 us (69%)
  blocking collectives  283 us (25%)
  matrix products  17.7 us (2%)
  other arithmetic  15.7 us (1%)
  between operations  13.2 us (1%)
  local copies, waits for them, and re-layouts  12.2 us (1%)
    psum x1, waiting for transfers between devices, shards(): lax.psum((second, row_spread, column_spread), 'dp')  367 us
    all_gather x1, waiting for transfers between devices, shards(): distance = jnp.sum(lax.all_gather(distance_part, 'mp'), axis=0)  326 us
    psum x1, blocking collectives, shards(): lax.psum((second, row_spread, column_spread), 'dp')  144 us
    psum x1, blocking collectives, shards(): lax.psum((jnp.sum(row_features.astype(jnp.float32), axis=0), jnp.sum(colu...  139 us
    all_gather x1, waiting for transfers between devices, shards(): landmark_piece = lax.all_gather(landmark_rows, 'dp', axis=1, tiled=True)  89.6 us
  transfers between devices with their start and end apart: 3, of which 3 were waited for; matrix products, arithmetic and copies ran while one was open for 0% of the time, Pallas kernels for 0%

profile of v1, /device:TPU:1, one launch (start us, length us, event | category | flops | bytes accessed | tf_op | source)
XLA Modules:
  0.0 1130.0 jit_solution(17074158252670107869)
XLA Ops:
  6.5 26.5 %while.10 = (s32[]{:T(128)}, bf16[8,512,128]{2,1,0:T(8,128)(2,1)S(1)}, s32[8]{0:T(128)S(1)}, bf16[512,1024]{1,0:T(8,128)(2,1)}, bf16[512,128]{1,0:T(8,128)(2,1)}...) while((s32[]{:T(128)}, bf16[8,512,128]{2,1,0:T(8,128)(2,1)S(1)}, ...), condition=%wide.region_4.5_spmd, body=%wide.region_1.4_spmd.sunk | while | flops 136641536 | bytes 4204739 | solution.py:50
  7.9 1.3 fusion.39
  9.9 0.7 dynamic_slice.34
  11.2 1.3 fusion.39
  13.2 0.7 dynamic_slice.34
  14.5 1.3 fusion.39
  16.5 0.7 dynamic_slice.34
  17.9 1.3 fusion.39
  21.2 1.3 fusion.39
  24.5 1.3 fusion.39
  27.8 1.3 fusion.39
  31.1 1.3 fusion.39
  36.8 89.6 %all-gather.3.cloned.1.call-done = bf16[2,512,1024]{2,1,0:T(8,128)(2,1)} async-done(((bf16[2,8,1024]{2,1,0:T(8,128)(2,1)}), bf16[2,512,1024]{2,1,0:T(8,128)(2,1)}) %all-gather.3.cloned.1.call-update) | async-done | bytes 2097168 | tf_op jit(solution)/shard_map/all_gather | solution.py:67
  126.4 2.1 convolution_bitcast_fusion
  128.5 0.7 convolution_bitcast_fusion.1
  130.0 1.9 copy.11
  132.6 326.1 %all-gather.5.cloned.1.call-done = f32[8,2,512,512]{3,2,1,0:T(8,128)} async-done(((f32[1,2,512,512]{3,2,1,0:T(8,128)}), f32[8,2,512,512]{3,2,1,0:T(8,128)}) %all-gather.5.cloned.1.call-update) | async-done | bytes 16777232 | tf_op jit(solution)/shard_map/all_gather | solution.py:73
  458.7 9.4 reduce_sum.84
  468.2 1.9 copy.14
  470.8 138.8 %all-reduce.1 = (f32[512]{0:T(512)S(1)}, f32[64]{0:T(128)S(1)}) all-reduce(f32[512]{0:T(512)S(1)} %convert_reduce_fusion, f32[64]{0:T(128)S(1)} %convert_reduce_fusion.1), channel_id=1, replica_groups=mesh['dp'=64,'mp'=8] {'dp'}, use_global_device_ids=true, to_apply=%region_11.13 | all-reduce | flops 576 | bytes 4608 | tf_op jit(solution)/shard_map/psum | solution.py:77
  610.2 1.1 fusion.13
  611.3 143.7 %all-reduce = (f32[512]{0:T(512)S(1)}, f32[64]{0:T(128)S(1)}) all-reduce(f32[512]{0:T(512)S(1)} %multiply_reduce_fusion.3, f32[64]{0:T(128)S(1)} %multiply_reduce_fusion.4), channel_id=1, replica_groups=mesh['dp'=64,'mp'=8] {'dp'}, use_global_device_ids=true, to_apply=%region_16.18 | all-reduce | flops 576 | bytes 4608 | tf_op jit(solution)/shard_map/psum | solution.py:89
  755.1 367.0 %all-reduce.4.cloned.1.call-done = f32[64,512]{0,1:T(8,128)} async-done(((f32[64,512]{0,1:T(8,128)}), f32[64,512]{0,1:T(8,128)}) %all-reduce.4.cloned.1.call-update) | async-done | bytes 131088 | tf_op jit(solution)/shard_map/psum | solution.py:89
  1122.1 1.3 rsqrt_multiply_fusion
  (78 shorter events, 14.9 us)
Async XLA Ops:
  6.5 119.8 %all-gather.3.cloned.1.call-start = ((), (), s32[]{:S(2)}) async-start(), calls=%async_computation | async-start | bytes 2129920 | tf_op jit(solution)/shard_map/all_gather | solution.py:67
  6.5 2.9 copy-start.4
  9.8 2.9 copy-start.4
  13.2 2.9 copy-start.4
  16.5 2.9 copy-start.4
  19.8 2.9 copy-start.4
  23.1 2.9 copy-start.4
  26.4 2.9 copy-start.4
  29.8 2.9 copy-start.4
  33.1 0.7 copy-start.5
  33.1 1.2 copy-start.1
  36.2 422.6 %all-gather.5.cloned.1.call-start = ((), (), s32[]{:S(2)}) async-start(), calls=%async_computation.1 | async-start | bytes 18874368 | tf_op jit(solution)/shard_map/all_gather | solution.py:73
  126.4 2.1 copy-start
  131.9 0.7 copy-start.2
  131.9 0.7 copy-start.3
  131.9 990.2 %all-reduce.4.cloned.1.call-start = ((), (), s32[]{:S(2)}) async-start(), calls=%async_computation.2 | async-start | bytes 524288 | tf_op jit(solution)/shard_map/psum | solution.py:89
Sparse Core Ops, SparseCore 0:
  36.3 90.0 all-gather.2
  132.0 326.6 all-gather.4
  611.4 510.6 all-reduce.3
